TPU v7x, 512 devices: a whole 4x4x16 slice. The times are simulated.
512 devices in a mesh: chol: 32 (over y, z_hi, x), pair: 16 (over z_lo, core).
Axes of the slice: x: 4, y: 4, z: 16 (z_hi: 2, z_lo: 8; z = z_hi * 8 + z_lo), core: 2. Of those that a mesh axis runs over, the one named last changes fastest.
Arguments:
- rotated: float32 [16384, 32768], P('chol', 'pair'), may hold values from -0.03125 to 0.03125
- green: float32 [1024, 32768], P('chol', 'pair'), may hold values from -6 to 6
- aux_field: float32 [1024, 16384], P('pair', 'chol'), may hold values from -6 to 6
Outputs:
- shifted: float32 [1024, 16384], P('pair', 'chol')
All inputs are finite; a program needn't handle non-finite values.
Results may differ from a plain program's by a relative error of at most 0.000056.
Values sent between devices are 32-bit elements; how exact they have to be, the bound alone decides.
No kernel may reach another device: no remote copies, remote signals or barrier semaphores. Data moves between devices by JAX's collectives and lax.ppermute only.
A program may use at most 64 MiB of HBM per device.

v0:
```python
import jax
import jax.numpy as jnp
from jax import lax
from jax.sharding import PartitionSpec as P

bias_cap = 1.5


def contract(rows, rotated):
    return lax.dot_general(
        rows,
        rotated,
        (((1,), (1,)), ((), ())),
        precision=lax.Precision.HIGHEST,
        preferred_element_type=jnp.float32,
    )


def body(rotated, green, aux_field):
    own_rows = aux_field.shape[0]
    gathered = contract(lax.all_gather(green, "chol", axis=0, tiled=True), rotated)
    total = lax.psum(gathered, "pair")
    share = lax.dynamic_slice_in_dim(total, lax.axis_index("pair") * own_rows, own_rows, 0)
    capped = jnp.clip(share, -bias_cap, bias_cap)
    return aux_field - capped


def solution(mesh):
    placed = (P("chol", "pair"), P("chol", "pair"), P("pair", "chol"))
    return jax.shard_map(
        body, mesh=mesh, in_specs=placed, out_specs=P("pair", "chol"), check_vma=False
    )
```

profile of v0, /device:TPU:14, one launch (start us, length us, event | category | flops | bytes accessed | tf_op | source)
XLA Modules:
  0.0 492.2 jit_solution(11579798569337451576)
XLA Ops:
  6.5 0.0 all-gather.2.cloned.1.call-start
  6.5 0.7 all-gather.2.cloned.1.call-update
  7.3 0.0 copy-start
  7.3 0.0 all-reduce.2.cloned.1.call-start
  7.3 252.7 %all-gather.2.cloned.1.call-done = f32[1024,2048]{1,0:T(8,128)} async-done(((f32[32,2048]{1,0:T(8,128)}), f32[1024,2048]{1,0:T(8,128)}) %all-gather.2.cloned.1.call-update) | async-done | bytes 8388624 | tf_op jit(solution)/shard_map/all_gather | solution.py:21
  260.0 17.1 %fusion = f32[1024,512]{1,0:T(8,128)} fusion(f32[1024,2048]{1,0:T(8,128)} %all-gather.2.cloned.1.call-done, f32[512,2048]{1,0:T(8,128)} %param.3), kind=kOutput, calls=%fused_computation.1 | convolution fusion | flops 12884901888 | bytes 14680064 | tf_op jit(solution)/shard_map/dot_general | solution.py:10
  277.1 0.0 all-reduce.2.cloned.1.call-update
  277.1 206.6 %all-reduce.2.cloned.1.call-done = f32[1024,512]{1,0:T(8,128)} async-done(((f32[1024,512]{1,0:T(8,128)}), f32[1024,512]{1,0:T(8,128)}) %all-reduce.2.cloned.1.call-update) | async-done | bytes 2097168 | tf_op jit(solution)/shard_map/psum | solution.py:22
  483.7 0.0 copy-done
  483.7 1.6 clamp_subtract_fusion
Async XLA Ops:
  6.5 253.5 %all-gather.2.cloned.1.call-start = ((), (), s32[]{:S(2)}) async-start(), calls=%async_computation | async-start | bytes 8650752 | tf_op jit(solution)/shard_map/all_gather | solution.py:21
  7.3 476.5 %copy-start = (f32[64,512]{1,0:T(8,128)S(1)}, f32[64,512]{1,0:T(8,128)}, u32[]{:S(2)}) copy-start(f32[64,512]{1,0:T(8,128)} %param.5) | copy-start | bytes 393220
  7.3 476.5 %all-reduce.2.cloned.1.call-start = ((), (), s32[]{:S(2)}) async-start(), calls=%async_computation.1 | async-start | bytes 4194304 | tf_op jit(solution)/shard_map/psum | solution.py:22
Sparse Core Ops, SparseCore 0:
  11.7 248.2 all-gather.1
  277.2 206.4 all-reduce.1
where the time goes:
time: 492 us
  waiting for transfers between devices  460 us (93%)
  matrix products  17.1 us (3%)
  between operations  13.4 us (3%)
    all_gather x1, waiting for transfers between devices, body(): lax.all_gather(green, 'chol', axis=0, tiled=True)  253 us
    psum x1, waiting for transfers between devices, body(): total = lax.psum(gathered, 'pair')  207 us
    dot_general x1, matrix products, contract(): lax.dot_general(rows, rotated, (((1,), (1,)), ((), ())), precision=lax.Pr...  17.1 us
  transfers between devices with their start and end apart: 2, of which 2 were waited for; matrix products, arithmetic and copies ran while one was open for 0% of the time, Pallas kernels for 0%

commit v1 on v0

--- a/solution.py
+++ b/solution.py
@@ -19,7 +19,8 @@
 def body(rotated, green, aux_field):
     own_rows = aux_field.shape[0]
     gathered = contract(lax.all_gather(green, "chol", axis=0, tiled=True), rotated)
-    total = lax.psum(gathered, "pair")
+    squares_list = lambda view: jnp.sum(lax.all_gather(view, axis_name="pair"), axis=0)
+    total = squares_list(gathered)
     share = lax.dynamic_slice_in_dim(total, lax.axis_index("pair") * own_rows, own_rows, 0)
     capped = jnp.clip(share, -bias_cap, bias_cap)
     return aux_field - capped

time: 492 us -> 662 us (1.35)
  the two profiles are of different devices: /device:TPU:14 before, /device:TPU:2 now
where the time goes in v1:
time: 662 us; the launch traced here: 661 us
  waiting for transfers between devices  617 us (93%)
  matrix products  17.1 us (3%)
  other arithmetic  13.4 us (2%)
  between operations  13.4 us (2%)
    all_gather x1, waiting for transfers between devices, body(): lax.all_gather(view, axis_name='pair')  363 us
    all_gather x1, waiting for transfers between devices, body(): lax.all_gather(green, 'chol', axis=0, tiled=True)  253 us
    dot_general x1, matrix products, contract(): lax.dot_general(rows, rotated, (((1,), (1,)), ((), ())), precision=lax.Pr...  17.1 us
  transfers between devices with their start and end apart: 2, of which 2 were waited for; matrix products, arithmetic and copies ran while one was open for 0% of the time, Pallas kernels for 0%

profile of v1, /device:TPU:2, one launch (start us, length us, event | category | flops | bytes accessed | tf_op | source)
XLA Modules:
  0.0 661.4 jit_solution(6305187999962749164)
XLA Ops:
  6.5 0.0 all-gather.4.cloned.1.call-start
  6.5 0.7 all-gather.4.cloned.1.call-update
  7.3 0.0 all-gather.6.cloned.1.call-start
  7.3 253.3 %all-gather.4.cloned.1.call-done = f32[1024,2048]{1,0:T(8,128)} async-done(((f32[32,2048]{1,0:T(8,128)}), f32[1024,2048]{1,0:T(8,128)}) %all-gather.4.cloned.1.call-update) | async-done | bytes 8388624 | tf_op jit(solution)/shard_map/all_gather | solution.py:21
  260.6 17.1 %fusion = f32[1024,512]{1,0:T(8,128)} fusion(f32[1024,2048]{1,0:T(8,128)} %all-gather.4.cloned.1.call-done, f32[512,2048]{1,0:T(8,128)} %param.3), kind=kOutput, calls=%fused_computation.1 | convolution fusion | flops 12884901888 | bytes 14680064 | tf_op jit(solution)/shard_map/dot_general | solution.py:10
  277.7 0.0 all-gather.6.cloned.1.call-update
  277.7 363.5 %all-gather.6.cloned.1.call-done = f32[16384,512]{1,0:T(8,128)} async-done(((f32[1024,512]{1,0:T(8,128)}), f32[16384,512]{1,0:T(8,128)}) %all-gather.6.cloned.1.call-update) | async-done | bytes 33554448 | tf_op jit(solution)/shard_map/all_gather | solution.py:22
  641.2 0.0 copy-start
  641.2 12.7 %reduce_sum.9 = f32[1024,512]{1,0:T(8,128)S(1)} reduce(f32[16,1024,512]{2,1,0:T(8,128)} %bitcast.3, f32[]{:T(128)} %constant.1.clone.1), dimensions={0}, to_apply=%region_0.0 | reduce | flops 7864320 | bytes 35651588 | tf_op jit(solution)/shard_map/reduce_sum | solution.py:22
  653.9 0.0 copy-done
  653.9 0.7 clamp_subtract_fusion
Async XLA Ops:
  6.5 254.0 %all-gather.4.cloned.1.call-start = ((), (), s32[]{:S(2)}) async-start(), calls=%async_computation | async-start | bytes 8650752 | tf_op jit(solution)/shard_map/all_gather | solution.py:21
  7.3 633.9 %all-gather.6.cloned.1.call-start = ((), (), s32[]{:S(2)}) async-start(), calls=%async_computation.1 | async-start | bytes 35651584 | tf_op jit(solution)/shard_map/all_gather | solution.py:22
  641.2 12.7 %copy-start = (f32[64,512]{1,0:T(8,128)S(1)}, f32[64,512]{1,0:T(8,128)}, u32[]{:S(2)}) copy-start(f32[64,512]{1,0:T(8,128)} %param.5) | copy-start | bytes 393220
Sparse Core Ops, SparseCore 0:
  11.7 248.7 all-gather.3
  277.8 363.2 all-gather.5
